TPU v7x, 32 devices: a whole 2x2x4 slice. The times are simulated.
32 devices in a mesh: groups: 2 (over y), dp: 4 (over z), task: 4 (over x, core).
Axes of the slice: x: 2, y: 2, z: 4, core: 2. Of those that a mesh axis runs over, the one named last changes fastest.
Arguments:
- coords: bfloat16 [3, 6144], P(None, ('groups', 'dp')), parts along dimension 1, may hold values from 0 to 1
- lengthscales: float32 [6], P('groups'), parts along dimension 0, may hold values from 0.15 to 0.5
- vectors: bfloat16 [2, 6144, 256], P(None, ('groups', 'dp'), 'task'), parts along dimension 1, may hold values from -6 to 6
- mixing: bfloat16 [512, 256], P('groups'), parts along dimension 0, may hold values from -0.078125 to 0.078125
- noise: float32 [512], P(('groups', 'task')), parts along dimension 0, may hold values from 0.1 to 1
Outputs:
- product: bfloat16 [2, 6144, 256], P(None, ('groups', 'dp'), 'task'), parts along dimension 1
- gradient: float32 [512, 256], P(('groups', 'task')), parts along dimension 0
There are 2 independent parts, one for each index of `groups`. A program takes and returns all parts, laid end to end along the dimension named above; each array names one. Nothing has to cross between parts.
All inputs are finite; a program needn't handle non-finite values.
Results may differ from a plain program's by a relative error of at most 0.0056.
Values may be sent and summed in bfloat16 or wider, within the bound.
No kernel may reach another device: no remote copies, remote signals or barrier semaphores. Data moves between devices by JAX's collectives and lax.ppermute only.
A program may use at most 64 MiB of HBM per device.

v0:
```python
import jax
import jax.numpy as jnp
from jax import lax
from jax.sharding import PartitionSpec as P


def kernel_tile(left, right):
    diff = left[:, :, None] - right[:, None, :]
    return jnp.exp(0.1 - jnp.sqrt(jnp.sum(diff * diff, axis=0) + 0.01))


def shift(x, axis, k, n):
    return lax.ppermute(x, axis, [(i, (i + k) % n) for i in range(n)])


def sum_over(x, axis, n):
    if n == 4:
        got = [shift(x, axis, k, n) for k in range(1, n)]
        even = lax.axis_index(axis) % 2 == 0
        first = x + jnp.where(even, got[2], got[0])
        second = got[1] + jnp.where(even, got[0], got[2])
        return first + second
    if n & n - 1:
        return lax.psum(x, axis)
    step = 1
    while step < n:
        x = x + lax.ppermute(x, axis, [(i, i ^ step) for i in range(n)])
        step *= 2
    return x


def per_device(coords, lengthscales, vectors, mixing, noise):
    n_rows = coords.shape[1]
    local_tasks = vectors.shape[2]
    n_dp = lax.axis_size("dp")
    task_start = lax.axis_index("task") * local_tasks
    inverse = 1.0 / lengthscales
    own_scaled = coords.astype(jnp.float32) * inverse[:, None]

    def block(right_coords, values):
        right = right_coords.astype(jnp.float32) * inverse[:, None]
        tile = kernel_tile(own_scaled, right).astype(jnp.bfloat16)
        return jnp.einsum("nr,srm->snm", tile, values, preferred_element_type=jnp.float32)

    task_input = vectors
    if n_dp <= 4:
        moved = [shift(vectors, "dp", k, n_dp) for k in range(1, n_dp)]
        if n_dp == 4:
            first = shift(coords, "dp", 1, n_dp)
            peer_coords = [first, shift(first, "dp", 1, n_dp), shift(coords, "dp", 3, n_dp)]
        else:
            peer_coords = [shift(coords, "dp", k, n_dp) for k in range(1, n_dp)]
        task_input = lax.optimization_barrier((vectors, peer_coords))[0]
        summed = block(coords, vectors)
        order = [1, 3, 2] if n_dp == 4 else list(range(1, n_dp))
        for k in order:
            summed = summed + block(peer_coords[k - 1], moved[k - 1])
    else:

        def ring(_, carry):
            accum, right_coords, values = carry
            right_coords = shift(right_coords, "dp", 1, n_dp)
            values = shift(values, "dp", 1, n_dp)
            return (accum + block(right_coords, values), right_coords, values)

        summed = block(coords, vectors)
        summed = lax.fori_loop(0, n_dp - 1, ring, (summed, coords, vectors))[0]
    n_task = lax.axis_size("task")
    copies = jnp.broadcast_to(task_input[None], (n_task,) + vectors.shape)
    task_blocks = lax.all_to_all(copies, "task", 0, 0, tiled=True)
    images = summed.astype(jnp.bfloat16)
    signs = jnp.array([1.0, -1.0], jnp.bfloat16)
    signed = images * signs[:, None, None]
    partial_grad = jnp.einsum(
        "sna,ksnb->akb", signed, task_blocks, preferred_element_type=jnp.float32
    ).reshape(local_tasks, n_task * local_tasks)
    total = sum_over(partial_grad, "dp", n_dp)
    gather_input = lax.optimization_barrier((images, task_blocks))[0]
    whole_images = lax.all_gather(
        jnp.transpose(gather_input, (2, 0, 1)), "task", axis=0, tiled=True
    )
    own_rows = lax.dynamic_slice_in_dim(mixing, task_start, local_tasks, 0)
    mixed = jnp.einsum("asn,ca->snc", whole_images, own_rows, preferred_element_type=jnp.float32)
    product = (mixed + noise[None, None, :] * vectors.astype(jnp.float32)).astype(jnp.bfloat16)
    gradient = total / (2.0 * n_rows * n_dp)
    return (product, gradient)


def solution(mesh):
    in_specs = (
        P(None, ("groups", "dp")),
        P("groups"),
        P(None, ("groups", "dp"), "task"),
        P("groups", None),
        P(("groups", "task")),
    )
    out_specs = (P(None, ("groups", "dp"), "task"), P(("groups", "task"), None))
    return jax.shard_map(
        per_device, mesh=mesh, in_specs=in_specs, out_specs=out_specs, check_vma=False
    )
```

profile of v0, /device:TPU:0, one launch (start us, length us, event | category | flops | bytes accessed | tf_op | source)
XLA Modules:
  0.0 54.8 jit_solution(17863950669732573691)
XLA Ops:
  0.7 3.1 %collective-permute-start = (bf16[3,768]{1,0:T(4,128)(2,1)}, bf16[3,768]{1,0:T(4,128)(2,1)S(1)}, u32[]{:S(2)}, u32[]{:S(2)}) collective-permute-start(bf16[3,768]{1,0:T(4,128)(2,1)} %param.6), channel_id=1, source_target_pairs={{0,4},{4,8},{8,12},{12,0},{1,5},{5,9},{9,13},{13,1},{2,6},{6,10},{... | collective-permute-start | bytes 13832 | tf_op jit(solution)/shard_map/ppermute | solution.py:13
  3.7 2.1 %collective-permute-start.2 = (bf16[3,768]{1,0:T(4,128)(2,1)}, bf16[3,768]{1,0:T(4,128)(2,1)S(1)}, u32[]{:S(2)}, u32[]{:S(2)}) collective-permute-start(bf16[3,768]{1,0:T(4,128)(2,1)} %param.6), channel_id=1, source_target_pairs={{0,12},{4,0},{8,4},{12,8},{1,13},{5,1},{9,5},{13,9},{2,14},{6,2},{... | collective-permute-start | bytes 13832 | tf_op jit(solution)/shard_map/ppermute | solution.py:13
  5.8 3.8 %collective-permute-start.3 = (bf16[2,768,64]{1,2,0:T(8,128)(2,1)}, bf16[2,768,64]{1,2,0:T(8,128)(2,1)S(1)}, u32[]{:S(2)}, u32[]{:S(2)}) collective-permute-start(bf16[2,768,64]{1,2,0:T(8,128)(2,1)} %param.8), channel_id=1, source_target_pairs={{0,12},{4,0},{8,4},{12,8},{1,13},{5,1},{9,5},{13,9},{2,14},{6,2},{... | collective-permute-start | bytes 589832 | tf_op jit(solution)/shard_map/ppermute | solution.py:13
  9.7 0.7 %collective-permute-start.4 = (bf16[3,768]{1,0:T(4,128)(2,1)S(1)}, bf16[3,768]{1,0:T(4,128)(2,1)S(1)}, u32[]{:S(2)}, u32[]{:S(2)}) collective-permute-start(bf16[3,768]{1,0:T(4,128)(2,1)S(1)} %collective-permute-done), channel_id=1, source_target_pairs={{0,4},{4,8},{8,12},{12,0},{1,5},{5,9},{9,13},{13,1},{2,6},{6,10},{... | collective-permute-start | bytes 13832 | tf_op jit(solution)/shard_map/ppermute | solution.py:13
  10.4 0.7 %broadcast_divide_fusion = f32[3]{0:T(128)S(1)} fusion(f32[3]{0:T(128)} %param.7), kind=kLoop, calls=%fused_computation.28 | loop fusion | flops 3 | bytes 24 | tf_op jit(solution)/shard_map/div | solution.py:37
  11.0 11.9 %collective-permute-done.4 = bf16[3,768]{1,0:T(4,128)(2,1)S(1)} collective-permute-done((bf16[3,768]{1,0:T(4,128)(2,1)S(1)}, bf16[3,768]{1,0:T(4,128)(2,1)S(1)}, u32[]{:S(2)}, u32[]{:S(2)}) %collective-permute-start.4) | collective-permute-done | bytes 4640 | tf_op jit(solution)/shard_map/ppermute | solution.py:13
  22.9 1.9 %broadcast_in_dim.2 = bf16[4,2,768,64]{2,3,1,0:T(8,128)(2,1)} broadcast(bf16[2,768,64]{1,2,0:T(8,128)(2,1)} %param.8), dimensions={1,2,3} | broadcast | bytes 983040 | tf_op jit(solution)/shard_map/broadcast_in_dim | solution.py:69
  24.8 3.5 %all-to-all-start = ((bf16[4,2,768,64]{2,3,1,0:T(8,128)(2,1)}), bf16[4,2,768,64]{2,3,1,0:T(8,128)(2,1)S(1)}, u32[]{:S(2)}, u32[]{:S(2)}) async-start(bf16[4,2,768,64]{2,3,1,0:T(8,128)(2,1)} %broadcast_in_dim.2), calls=%async_computation | async-start | bytes 1572864 | tf_op jit(solution)/shard_map/all_to_all | solution.py:70
  28.3 0.1 convert_multiply_fusion
  28.4 4.7 %multiply_reduce_fusion.2 = (f32[768,768]{1,0:T(8,128)S(1)}, f32[768,768]{1,0:T(8,128)S(1)}, f32[768,768]{1,0:T(8,128)S(1)}, f32[768,768]{1,0:T(8,128)S(1)}) fusion(f32[3,768]{1,0:T(4,128)S(1)} %get-tuple-element.11, f32[3,768]{1,0:T(4,128)S(1)} %get-tuple-element.13, f32[3,768]{1,0:T(4,128)S(1)} %get-tuple-element.12, f32[3,768]{1,0:T(4,128)S(1)} %get-tuple-element.10), kind=kLoop, calls=%fused_computation.2 | loop fusion | flops 18874368 | bytes 9474048 | tf_op jit(solution)/shard_map/reduce_sum | solution.py:9
  33.0 1.1 %fusion = f32[768,128]{0,1:S(1)} fusion(bf16[768,128]{0,1:T(8,128)(2,1)S(1)} %bitcast.35, f32[768,768]{1,0:T(8,128)S(1)} %get-tuple-element.9), kind=kOutput, calls=%fused_computation.9 | convolution fusion | flops 152764416 | bytes 2949120
  34.1 1.1 %fusion.1 = f32[768,128]{0,1:S(1)} fusion(bf16[768,128]{0,1:T(8,128)(2,1)S(1)} %bitcast.42, f32[768,768]{1,0:T(8,128)S(1)} %get-tuple-element.6), kind=kOutput, calls=%fused_computation.10 | convolution fusion | flops 152764416 | bytes 2949120
  35.2 1.1 %fusion.2 = f32[768,128]{0,1:S(1)} fusion(bf16[768,128]{0,1:T(8,128)(2,1)S(1)} %bitcast.41, f32[768,768]{1,0:T(8,128)S(1)} %get-tuple-element.7), kind=kOutput, calls=%fused_computation.11 | convolution fusion | flops 152764416 | bytes 2949120
  36.4 1.1 %fusion.3 = f32[768,128]{0,1:S(1)} fusion(bf16[768,128]{0,1:T(8,128)(2,1)S(1)} %bitcast.40, f32[768,768]{1,0:T(8,128)S(1)} %get-tuple-element.8), kind=kOutput, calls=%fused_computation.12 | convolution fusion | flops 152764416 | bytes 2949120
  37.5 0.1 fusion.5
  37.6 2.3 %all-to-all-done = bf16[4,2,768,64]{2,3,1,0:T(8,128)(2,1)S(1)} async-done(((bf16[4,2,768,64]{2,3,1,0:T(8,128)(2,1)}), bf16[4,2,768,64]{2,3,1,0:T(8,128)(2,1)S(1)}, u32[]{:S(2)}, u32[]{:S(2)}) %all-to-all-start) | async-done | bytes 786464 | tf_op jit(solution)/shard_map/all_to_all | solution.py:70
  39.9 0.5 convolution_bitcast_fusion
  40.4 0.1 copy.9
  40.5 0.1 reshape.16
  40.7 2.0 %collective-permute-start.7 = (f32[64,256]{1,0:T(8,128)S(1)}, f32[64,256]{1,0:T(8,128)S(1)}, u32[]{:S(2)}, u32[]{:S(2)}) collective-permute-start(f32[64,256]{1,0:T(8,128)S(1)} %reshape.16), channel_id=1, source_target_pairs={{0,4},{4,8},{8,12},{12,0},{1,5},{5,9},{9,13},{13,1},{2,6},{6,10},{... | collective-permute-start | bytes 196616 | tf_op jit(solution)/shard_map/ppermute | solution.py:13
  42.7 3.1 %collective-permute-start.8 = (f32[64,256]{1,0:T(8,128)S(1)}, f32[64,256]{1,0:T(8,128)S(1)}, u32[]{:S(2)}, u32[]{:S(2)}) collective-permute-start(f32[64,256]{1,0:T(8,128)S(1)} %reshape.16), channel_id=1, source_target_pairs={{0,8},{4,12},{8,0},{12,4},{1,9},{5,13},{9,1},{13,5},{2,10},{6,14},... | collective-permute-start | bytes 196616 | tf_op jit(solution)/shard_map/ppermute | solution.py:13
  45.8 7.4 %all_gather.3 = bf16[256,2,768]{2,0,1:T(8,128)(2,1)S(1)} all-gather(bf16[64,2,768]{2,0,1:T(8,128)(2,1)S(1)} %bitcast.34), channel_id=1, replica_groups=mesh['groups'=2,'dp'=4,'task'=4] {'task'}, dimensions={0}, use_global_device_ids=true | all-gather | bytes 983040 | tf_op jit(solution)/shard_map/all_gather | solution.py:79
  53.2 0.9 %fusion.4 = bf16[2,768,64]{1,2,0:T(8,128)(2,1)} fusion(bf16[256,2,768]{2,0,1:T(8,128)(2,1)S(1)} %all_gather.3, bf16[2,768,64]{1,2,0:T(8,128)(2,1)S(1)} %copy-done.1, f32[64]{0:T(128)S(1)} %copy-done.3, bf16[256,256]{1,0:T(8,128)(2,1)S(1)} %copy-done, s32[]{:T(128)S(6)} %select_n.22), kind=kOutput, calls=%fused_computation.13 | convolution fusion | flops 50724864 | bytes 1212932 | tf_op jit(solution)/shard_map/asn,ca->snc/dot_general | solution.py:83
  54.2 0.7 %add_multiply_fusion = f32[64,256]{1,0:T(8,128)} fusion(f32[64,256]{1,0:T(8,128)S(1)} %collective-permute-done.8, f32[64,256]{1,0:T(8,128)S(1)} %collective-permute-done.7, f32[64,256]{1,0:T(8,128)S(1)} %collective-permute-done.6, f32[64,256]{1,0:T(8,128)S(1)} %reshape.16, pred[]{:T(512)S(6)} %eq.5), kind=kLoop, calls=%fused_computation.20 | loop fusion | flops 98304 | bytes 327681 | tf_op jit(solution)/shard_map/div | solution.py:85
  (21 shorter events, 0.1 us)
Async XLA Ops:
  0.6 52.6 %copy-start = (bf16[256,256]{1,0:T(8,128)(2,1)S(1)}, bf16[256,256]{1,0:T(8,128)(2,1)}, u32[]{:S(2)}) copy-start(bf16[256,256]{1,0:T(8,128)(2,1)} %param.9) | copy-start | bytes 393220
  0.6 27.6 %copy-start.2 = (bf16[3,768]{1,0:T(4,128)(2,1)S(1)}, bf16[3,768]{1,0:T(4,128)(2,1)}, u32[]{:S(2)}) copy-start(bf16[3,768]{1,0:T(4,128)(2,1)} %param.6) | copy-start | bytes 13828
  0.7 9.0 %collective-permute-start = (bf16[3,768]{1,0:T(4,128)(2,1)}, bf16[3,768]{1,0:T(4,128)(2,1)S(1)}, u32[]{:S(2)}, u32[]{:S(2)}) collective-permute-start(bf16[3,768]{1,0:T(4,128)(2,1)} %param.6), channel_id=1, source_target_pairs={{0,4},{4,8},{8,12},{12,0},{1,5},{5,9},{9,13},{13,1},{2,6},{6,10},{... | collective-permute-start | bytes 13832 | tf_op jit(solution)/shard_map/ppermute | solution.py:13
  3.7 7.3 %collective-permute-start.2 = (bf16[3,768]{1,0:T(4,128)(2,1)}, bf16[3,768]{1,0:T(4,128)(2,1)S(1)}, u32[]{:S(2)}, u32[]{:S(2)}) collective-permute-start(bf16[3,768]{1,0:T(4,128)(2,1)} %param.6), channel_id=1, source_target_pairs={{0,12},{4,0},{8,4},{12,8},{1,13},{5,1},{9,5},{13,9},{2,14},{6,2},{... | collective-permute-start | bytes 13832 | tf_op jit(solution)/shard_map/ppermute | solution.py:13
  5.8 28.3 %collective-permute-start.1 = (bf16[2,768,64]{1,2,0:T(8,128)(2,1)}, bf16[2,768,64]{1,2,0:T(8,128)(2,1)S(1)}, u32[]{:S(2)}, u32[]{:S(2)}) collective-permute-start(bf16[2,768,64]{1,2,0:T(8,128)(2,1)} %param.8), channel_id=1, source_target_pairs={{0,4},{4,8},{8,12},{12,0},{1,5},{5,9},{9,13},{13,1},{2,6},{6,10},{... | collective-permute-start | bytes 589832 | tf_op jit(solution)/shard_map/ppermute | solution.py:13
  5.8 29.4 %collective-permute-start.3 = (bf16[2,768,64]{1,2,0:T(8,128)(2,1)}, bf16[2,768,64]{1,2,0:T(8,128)(2,1)S(1)}, u32[]{:S(2)}, u32[]{:S(2)}) collective-permute-start(bf16[2,768,64]{1,2,0:T(8,128)(2,1)} %param.8), channel_id=1, source_target_pairs={{0,12},{4,0},{8,4},{12,8},{1,13},{5,1},{9,5},{13,9},{2,14},{6,2},{... | collective-permute-start | bytes 589832 | tf_op jit(solution)/shard_map/ppermute | solution.py:13
  9.6 26.7 %collective-permute-start.5 = (bf16[2,768,64]{1,2,0:T(8,128)(2,1)}, bf16[2,768,64]{1,2,0:T(8,128)(2,1)S(1)}, u32[]{:S(2)}, u32[]{:S(2)}) collective-permute-start(bf16[2,768,64]{1,2,0:T(8,128)(2,1)} %param.8), channel_id=1, source_target_pairs={{0,8},{4,12},{8,0},{12,4},{1,9},{5,13},{9,1},{13,5},{2,10},{6,14},... | collective-permute-start | bytes 589832 | tf_op jit(solution)/shard_map/ppermute | solution.py:13
  9.7 13.2 %collective-permute-start.4 = (bf16[3,768]{1,0:T(4,128)(2,1)S(1)}, bf16[3,768]{1,0:T(4,128)(2,1)S(1)}, u32[]{:S(2)}, u32[]{:S(2)}) collective-permute-start(bf16[3,768]{1,0:T(4,128)(2,1)S(1)} %collective-permute-done), channel_id=1, source_target_pairs={{0,4},{4,8},{8,12},{12,0},{1,5},{5,9},{9,13},{13,1},{2,6},{6,10},{... | collective-permute-start | bytes 13832 | tf_op jit(solution)/shard_map/ppermute | solution.py:13
  24.8 15.1 %all-to-all-start = ((bf16[4,2,768,64]{2,3,1,0:T(8,128)(2,1)}), bf16[4,2,768,64]{2,3,1,0:T(8,128)(2,1)S(1)}, u32[]{:S(2)}, u32[]{:S(2)}) async-start(bf16[4,2,768,64]{2,3,1,0:T(8,128)(2,1)} %broadcast_in_dim.2), calls=%async_computation | async-start | bytes 1572864 | tf_op jit(solution)/shard_map/all_to_all | solution.py:70
  28.4 4.7 %copy-start.1 = (bf16[2,768,64]{1,2,0:T(8,128)(2,1)S(1)}, bf16[2,768,64]{1,2,0:T(8,128)(2,1)}, u32[]{:S(2)}) copy-start(bf16[2,768,64]{1,2,0:T(8,128)(2,1)} %param.8) | copy-start | bytes 589828
  36.4 3.5 %copy-start.4 = (bf16[2]{0:T(256)(128)(2,1)S(1)}, bf16[2]{0:T(256)(128)(2,1)}, u32[]{:S(2)}) copy-start(bf16[2]{0:T(256)(128)(2,1)} %constant.38.clone) | copy-start | bytes 16
  37.5 15.8 %copy-start.3 = (f32[64]{0:T(128)S(1)}, f32[64]{0:T(128)}, u32[]{:S(2)}) copy-start(f32[64]{0:T(128)} %param.10) | copy-start | bytes 772
  40.6 13.5 %collective-permute-start.6 = (f32[64,256]{1,0:T(8,128)S(1)}, f32[64,256]{1,0:T(8,128)S(1)}, u32[]{:S(2)}, u32[]{:S(2)}) collective-permute-start(f32[64,256]{1,0:T(8,128)S(1)} %reshape.16), channel_id=1, source_target_pairs={{0,12},{4,0},{8,4},{12,8},{1,13},{5,1},{9,5},{13,9},{2,14},{6,2},{... | collective-permute-start | bytes 196616 | tf_op jit(solution)/shard_map/ppermute | solution.py:13
  40.7 13.5 %collective-permute-start.7 = (f32[64,256]{1,0:T(8,128)S(1)}, f32[64,256]{1,0:T(8,128)S(1)}, u32[]{:S(2)}, u32[]{:S(2)}) collective-permute-start(f32[64,256]{1,0:T(8,128)S(1)} %reshape.16), channel_id=1, source_target_pairs={{0,4},{4,8},{8,12},{12,0},{1,5},{5,9},{9,13},{13,1},{2,6},{6,10},{... | collective-permute-start | bytes 196616 | tf_op jit(solution)/shard_map/ppermute | solution.py:13
  42.7 11.5 %collective-permute-start.8 = (f32[64,256]{1,0:T(8,128)S(1)}, f32[64,256]{1,0:T(8,128)S(1)}, u32[]{:S(2)}, u32[]{:S(2)}) collective-permute-start(f32[64,256]{1,0:T(8,128)S(1)} %reshape.16), channel_id=1, source_target_pairs={{0,8},{4,12},{8,0},{12,4},{1,9},{5,13},{9,1},{13,5},{2,10},{6,14},... | collective-permute-start | bytes 196616 | tf_op jit(solution)/shard_map/ppermute | solution.py:13
where the time goes:
time: 55.1 us; the launch traced here: 54.8 us
  starting transfers between devices  18.3 us (33%)
  waiting for transfers between devices  14.2 us (26%)
  blocking collectives  7.45 us (14%)
  other arithmetic  6.12 us (11%)
  matrix products  5.86 us (11%)
  local copies, waits for them, and re-layouts  2.13 us (4%)
  between operations  0.74 us (1%)
    ppermute x9, starting transfers between devices, shift(): return lax.ppermute(x, axis, [(i, (i + k) % n) for i in range(n)])  14.8 us
    ppermute x9, waiting for transfers between devices, shift(): return lax.ppermute(x, axis, [(i, (i + k) % n) for i in range(n)])  11.9 us
    all_gather x1, blocking collectives, per_device(): lax.all_gather(jnp.transpose(gather_input, (2, 0, 1)), 'task', axis=0, ti...  7.45 us
    reduce_sum x1, other arithmetic, kernel_tile(): return jnp.exp(0.1 - jnp.sqrt(jnp.sum(diff * diff, axis=0) + 0.01))  4.65 us
    unnamed x4, matrix products  4.41 us
    all_to_all x1, starting transfers between devices, per_device(): task_blocks = lax.all_to_all(copies, 'task', 0, 0, tiled=True)  3.49 us
    all_to_all x1, waiting for transfers between devices, per_device(): task_blocks = lax.all_to_all(copies, 'task', 0, 0, tiled=True)  2.32 us
    broadcast_in_dim x1, local copies, waits for them, and re-layouts, per_device(): copies = jnp.broadcast_to(task_input[None], (n_task,) + vectors.shape)  1.87 us
  transfers between devices with their start and end apart: 10, of which 2 were waited for; matrix products, arithmetic and copies ran while one was open for 23% of the time, Pallas kernels for 0%

commit v1 on v0

--- a/solution.py
+++ b/solution.py
@@ -2,6 +2,23 @@
 import jax.numpy as jnp
 from jax import lax
 from jax.sharding import PartitionSpec as P
+
+
+def joined_along(blocks, dim):
+    blocks = jnp.moveaxis(blocks, 0, dim)
+    shape = blocks.shape
+    return blocks.reshape(*shape[:dim], shape[dim] * shape[dim + 1], *shape[dim + 2 :])
+
+
+def gather_around(x, axis, dim):
+    size = lax.axis_size(axis)
+    right = [(i, (i + 1) % size) for i in range(size)]
+    tiles = [x]
+    while len(tiles) < size:
+        tiles.append(lax.ppermute(tiles[-1], axis, right))
+    position = lax.axis_index(axis)
+    tiles = jnp.stack(tiles)[(position - jnp.arange(size)) % size]
+    return joined_along(tiles, dim)
 
 
 def kernel_tile(left, right):
@@ -76,9 +93,7 @@
     ).reshape(local_tasks, n_task * local_tasks)
     total = sum_over(partial_grad, "dp", n_dp)
     gather_input = lax.optimization_barrier((images, task_blocks))[0]
-    whole_images = lax.all_gather(
-        jnp.transpose(gather_input, (2, 0, 1)), "task", axis=0, tiled=True
-    )
+    whole_images = gather_around(jnp.transpose(gather_input, (2, 0, 1)), "task", 0)
     own_rows = lax.dynamic_slice_in_dim(mixing, task_start, local_tasks, 0)
     mixed = jnp.einsum("asn,ca->snc", whole_images, own_rows, preferred_element_type=jnp.float32)
     product = (mixed + noise[None, None, :] * vectors.astype(jnp.float32)).astype(jnp.bfloat16)

time: 55.1 us -> 58.9 us (1.069)
  waiting for transfers between devices: 14.2 us -> 23.7 us
  blocking collectives: 7.45 us -> 0 us
  starting transfers between devices: 18.3 us -> 19.3 us
  local copies, waits for them, and re-layouts: 2.13 us -> 2.77 us
    all_gather x1 -> x0, blocking collectives: 7.45 us -> none  [per_device(): lax.all_gather(jnp.transpose(gather_input, (2, 0, 1)), 'task', axis=0, ti...]
    ppermute x0 -> x3, waiting for transfers between devices: none -> 6.44 us  [gather_around(): tiles.append(lax.ppermute(tiles[-1], axis, right))]
    ppermute x9, waiting for transfers between devices: 11.9 us -> 14.9 us  [shift(): return lax.ppermute(x, axis, [(i, (i + k) % n) for i in range(n)])]
    ppermute x9, starting transfers between devices: 14.8 us -> 15.8 us  [shift(): return lax.ppermute(x, axis, [(i, (i + k) % n) for i in range(n)])]
    gather x0 -> x2, local copies, waits for them, and re-layouts: none -> 0.65 us  [gather_around(): tiles = jnp.stack(tiles)[(position - jnp.arange(size)) % size]]
  transfers between devices with their start and end apart: 10 -> 13, of which waited for: 2 -> 6; matrix products, arithmetic and copies ran while one was open for 23% -> 22% of each run, Pallas kernels for 0% -> 0%
where the time goes in v1:
time: 58.9 us; the launch traced here: 58.7 us
  waiting for transfers between devices  23.7 us (40%)
  starting transfers between devices  19.3 us (33%)
  other arithmetic  6.24 us (11%)
  matrix products  5.84 us (10%)
  local copies, waits for them, and re-layouts  2.77 us (5%)
  between operations  0.77 us (1%)
    ppermute x9, starting transfers between devices, shift(): return lax.ppermute(x, axis, [(i, (i + k) % n) for i in range(n)])  15.8 us
    ppermute x9, waiting for transfers between devices, shift(): return lax.ppermute(x, axis, [(i, (i + k) % n) for i in range(n)])  14.9 us
    ppermute x3, waiting for transfers between devices, gather_around(): tiles.append(lax.ppermute(tiles[-1], axis, right))  6.44 us
    reduce_sum x1, other arithmetic, kernel_tile(): return jnp.exp(0.1 - jnp.sqrt(jnp.sum(diff * diff, axis=0) + 0.01))  4.65 us
    unnamed x4, matrix products  4.38 us
    all_to_all x1, starting transfers between devices, per_device(): task_blocks = lax.all_to_all(copies, 'task', 0, 0, tiled=True)  3.49 us
    all_to_all x1, waiting for transfers between devices, per_device(): task_blocks = lax.all_to_all(copies, 'task', 0, 0, tiled=True)  2.36 us
    broadcast_in_dim x1, local copies, waits for them, and re-layouts, per_device(): copies = jnp.broadcast_to(task_input[None], (n_task,) + vectors.shape)  1.86 us
  transfers between devices with their start and end apart: 13, of which 6 were waited for; matrix products, arithmetic and copies ran while one was open for 22% of the time, Pallas kernels for 0%

profile of v1, /device:TPU:0, one launch (start us, length us, event | category | flops | bytes accessed | tf_op | source)
XLA Modules:
  0.0 58.7 jit_solution(10898211522993841011)
XLA Ops:
  0.7 3.1 %collective-permute-start = (bf16[3,768]{1,0:T(4,128)(2,1)}, bf16[3,768]{1,0:T(4,128)(2,1)S(1)}, u32[]{:S(2)}, u32[]{:S(2)}) collective-permute-start(bf16[3,768]{1,0:T(4,128)(2,1)} %param.6), channel_id=1, source_target_pairs={{0,4},{4,8},{8,12},{12,0},{1,5},{5,9},{9,13},{13,1},{2,6},{6,10},{... | collective-permute-start | bytes 13832 | tf_op jit(solution)/shard_map/ppermute | solution.py:30
  3.7 2.1 %collective-permute-start.2 = (bf16[3,768]{1,0:T(4,128)(2,1)}, bf16[3,768]{1,0:T(4,128)(2,1)S(1)}, u32[]{:S(2)}, u32[]{:S(2)}) collective-permute-start(bf16[3,768]{1,0:T(4,128)(2,1)} %param.6), channel_id=1, source_target_pairs={{0,12},{4,0},{8,4},{12,8},{1,13},{5,1},{9,5},{13,9},{2,14},{6,2},{... | collective-permute-start | bytes 13832 | tf_op jit(solution)/shard_map/ppermute | solution.py:30
  5.8 3.8 %collective-permute-start.3 = (bf16[2,768,64]{1,2,0:T(8,128)(2,1)}, bf16[2,768,64]{1,2,0:T(8,128)(2,1)S(1)}, u32[]{:S(2)}, u32[]{:S(2)}) collective-permute-start(bf16[2,768,64]{1,2,0:T(8,128)(2,1)} %param.8), channel_id=1, source_target_pairs={{0,12},{4,0},{8,4},{12,8},{1,13},{5,1},{9,5},{13,9},{2,14},{6,2},{... | collective-permute-start | bytes 589832 | tf_op jit(solution)/shard_map/ppermute | solution.py:30
  9.7 0.7 %collective-permute-start.4 = (bf16[3,768]{1,0:T(4,128)(2,1)S(1)}, bf16[3,768]{1,0:T(4,128)(2,1)S(1)}, u32[]{:S(2)}, u32[]{:S(2)}) collective-permute-start(bf16[3,768]{1,0:T(4,128)(2,1)S(1)} %collective-permute-done), channel_id=1, source_target_pairs={{0,4},{4,8},{8,12},{12,0},{1,5},{5,9},{9,13},{13,1},{2,6},{6,10},{... | collective-permute-start | bytes 13832 | tf_op jit(solution)/shard_map/ppermute | solution.py:30
  10.4 0.7 %broadcast_divide_fusion = f32[3]{0:T(128)S(1)} fusion(f32[3]{0:T(128)} %param.7), kind=kLoop, calls=%fused_computation.37 | loop fusion | flops 3 | bytes 24 | tf_op jit(solution)/shard_map/div | solution.py:54
  11.0 11.9 %collective-permute-done.4 = bf16[3,768]{1,0:T(4,128)(2,1)S(1)} collective-permute-done((bf16[3,768]{1,0:T(4,128)(2,1)S(1)}, bf16[3,768]{1,0:T(4,128)(2,1)S(1)}, u32[]{:S(2)}, u32[]{:S(2)}) %collective-permute-start.4) | collective-permute-done | bytes 4640 | tf_op jit(solution)/shard_map/ppermute | solution.py:30
  22.9 1.9 %broadcast_in_dim.2 = bf16[4,2,768,64]{2,3,1,0:T(8,128)(2,1)} broadcast(bf16[2,768,64]{1,2,0:T(8,128)(2,1)} %param.8), dimensions={1,2,3} | broadcast | bytes 983040 | tf_op jit(solution)/shard_map/broadcast_in_dim | solution.py:86
  24.8 3.5 %all-to-all-start = ((bf16[4,2,768,64]{2,3,1,0:T(8,128)(2,1)}), bf16[4,2,768,64]{2,3,1,0:T(8,128)(2,1)S(1)}, u32[]{:S(2)}, u32[]{:S(2)}) async-start(bf16[4,2,768,64]{2,3,1,0:T(8,128)(2,1)} %broadcast_in_dim.2), calls=%async_computation | async-start | bytes 1572864 | tf_op jit(solution)/shard_map/all_to_all | solution.py:87
  28.4 4.7 %multiply_reduce_fusion.2 = (f32[768,768]{1,0:T(8,128)S(1)}, f32[768,768]{1,0:T(8,128)S(1)}, f32[768,768]{1,0:T(8,128)S(1)}, f32[768,768]{1,0:T(8,128)S(1)}) fusion(f32[3,768]{1,0:T(4,128)S(1)} %get-tuple-element.11, f32[3,768]{1,0:T(4,128)S(1)} %get-tuple-element.13, f32[3,768]{1,0:T(4,128)S(1)} %get-tuple-element.12, f32[3,768]{1,0:T(4,128)S(1)} %get-tuple-element.10), kind=kLoop, calls=%fused_computation.3 | loop fusion | flops 18874368 | bytes 9474048 | tf_op jit(solution)/shard_map/reduce_sum | solution.py:26
  33.0 1.1 %fusion = f32[768,128]{0,1:S(1)} fusion(bf16[768,128]{0,1:T(8,128)(2,1)S(1)} %bitcast.45, f32[768,768]{1,0:T(8,128)S(1)} %get-tuple-element.9), kind=kOutput, calls=%fused_computation.10 | convolution fusion | flops 152764416 | bytes 2949120
  34.1 1.1 %fusion.1 = f32[768,128]{0,1:S(1)} fusion(bf16[768,128]{0,1:T(8,128)(2,1)S(1)} %bitcast.55, f32[768,768]{1,0:T(8,128)S(1)} %get-tuple-element.6), kind=kOutput, calls=%fused_computation.11 | convolution fusion | flops 152764416 | bytes 2949120
  35.2 1.1 %fusion.2 = f32[768,128]{0,1:S(1)} fusion(bf16[768,128]{0,1:T(8,128)(2,1)S(1)} %bitcast.54, f32[768,768]{1,0:T(8,128)S(1)} %get-tuple-element.7), kind=kOutput, calls=%fused_computation.12 | convolution fusion | flops 152764416 | bytes 2949120
  36.3 1.1 %fusion.3 = f32[768,128]{0,1:S(1)} fusion(bf16[768,128]{0,1:T(8,128)(2,1)S(1)} %bitcast.53, f32[768,768]{1,0:T(8,128)S(1)} %get-tuple-element.8), kind=kOutput, calls=%fused_computation.13 | convolution fusion | flops 152764416 | bytes 2949120
  37.5 2.4 %all-to-all-done = bf16[4,2,768,64]{2,3,1,0:T(8,128)(2,1)S(1)} async-done(((bf16[4,2,768,64]{2,3,1,0:T(8,128)(2,1)}), bf16[4,2,768,64]{2,3,1,0:T(8,128)(2,1)S(1)}, u32[]{:S(2)}, u32[]{:S(2)}) %all-to-all-start) | async-done | bytes 786464 | tf_op jit(solution)/shard_map/all_to_all | solution.py:87
  39.9 5.1 %collective-permute-done.6 = bf16[64,2,768]{2,0,1:T(8,128)(2,1)S(1)} collective-permute-done((bf16[64,2,768]{2,0,1:T(8,128)(2,1)S(1)}, bf16[64,2,768]{2,0,1:T(8,128)(2,1)S(1)}, u32[]{:S(2)}, u32[]{:S(2)}) %collective-permute-start.6) | collective-permute-done | bytes 196640 | tf_op jit(solution)/shard_map/ppermute | solution.py:18
  45.0 0.5 convolution_bitcast_fusion
  45.7 1.2 %collective-permute-start.10 = (f32[64,256]{1,0:T(8,128)S(1)}, f32[64,256]{1,0:T(8,128)S(1)}, u32[]{:S(2)}, u32[]{:S(2)}) collective-permute-start(f32[64,256]{1,0:T(8,128)S(1)} %reshape.69), channel_id=1, source_target_pairs={{0,4},{4,8},{8,12},{12,0},{1,5},{5,9},{9,13},{13,1},{2,6},{6,10},{... | collective-permute-start | bytes 196616 | tf_op jit(solution)/shard_map/ppermute | solution.py:30
  47.0 2.0 %collective-permute-start.11 = (f32[64,256]{1,0:T(8,128)S(1)}, f32[64,256]{1,0:T(8,128)S(1)}, u32[]{:S(2)}, u32[]{:S(2)}) collective-permute-start(f32[64,256]{1,0:T(8,128)S(1)} %reshape.69), channel_id=1, source_target_pairs={{0,8},{4,12},{8,0},{12,4},{1,9},{5,13},{9,1},{13,5},{2,10},{6,14},... | collective-permute-start | bytes 196616 | tf_op jit(solution)/shard_map/ppermute | solution.py:30
  48.9 2.8 %collective-permute-start.9 = (f32[64,256]{1,0:T(8,128)S(1)}, f32[64,256]{1,0:T(8,128)S(1)}, u32[]{:S(2)}, u32[]{:S(2)}) collective-permute-start(f32[64,256]{1,0:T(8,128)S(1)} %reshape.69), channel_id=1, source_target_pairs={{0,12},{4,0},{8,4},{12,8},{1,13},{5,1},{9,5},{13,9},{2,14},{6,2},{... | collective-permute-start | bytes 196616 | tf_op jit(solution)/shard_map/ppermute | solution.py:30
  52.2 2.7 %collective-permute-done.11 = f32[64,256]{1,0:T(8,128)S(1)} collective-permute-done((f32[64,256]{1,0:T(8,128)S(1)}, f32[64,256]{1,0:T(8,128)S(1)}, u32[]{:S(2)}, u32[]{:S(2)}) %collective-permute-start.11) | collective-permute-done | bytes 65568 | tf_op jit(solution)/shard_map/ppermute | solution.py:30
  54.9 0.6 %add_multiply_fusion = f32[64,256]{1,0:T(8,128)} fusion(f32[64,256]{1,0:T(8,128)S(1)} %collective-permute-done.11, f32[64,256]{1,0:T(8,128)S(1)} %collective-permute-done.10, f32[64,256]{1,0:T(8,128)S(1)} %collective-permute-done.9, f32[64,256]{1,0:T(8,128)S(1)} %reshape.69, pred[]{:T(512)S(6)} %eq.7), kind=kLoop, calls=%fused_computation.22 | loop fusion | flops 98304 | bytes 327681 | tf_op jit(solution)/shard_map/div | solution.py:100
  55.6 1.4 %collective-permute-done.8 = bf16[64,2,768]{2,0,1:T(8,128)(2,1)S(1)} collective-permute-done((bf16[64,2,768]{2,0,1:T(8,128)(2,1)S(1)}, bf16[64,2,768]{2,0,1:T(8,128)(2,1)S(1)}, u32[]{:S(2)}, u32[]{:S(2)}) %collective-permute-start.8) | collective-permute-done | bytes 196640 | tf_op jit(solution)/shard_map/ppermute | solution.py:18
  57.0 0.6 %gather_fusion = bf16[4,64,2,768]{3,1,2,0:T(8,128)(2,1)S(1)} fusion(bf16[4,64,2,768]{3,1,2,0:T(8,128)(2,1)S(1)} %pad_maximum_fusion, s32[1024]{0:T(1024)S(1)} %pad_clamp_fusion), kind=kCustom, calls=%fused_computation | custom fusion | bytes 1572880 | tf_op jit(solution)/shard_map/gather | solution.py:20
  57.7 1.0 %fusion.4 = bf16[2,768,64]{1,2,0:T(8,128)(2,1)} fusion(bf16[256,2,768]{2,0,1:T(8,128)(2,1)S(1)} %bitcast.42, bf16[2,768,64]{1,2,0:T(8,128)(2,1)S(1)} %copy-done.1, f32[64]{0:T(128)S(1)} %copy-done.3, bf16[256,256]{1,0:T(8,128)(2,1)S(1)} %copy-done, s32[]{:T(128)S(6)} %select_n.47), kind=kOutput, calls=%fused_computation.14 | convolution fusion | flops 50724864 | bytes 1212932 | tf_op jit(solution)/shard_map/asn,ca->snc/dot_general | solution.py:98
  (31 shorter events, 1.0 us)
Async XLA Ops:
  0.6 57.1 %copy-start = (bf16[256,256]{1,0:T(8,128)(2,1)S(1)}, bf16[256,256]{1,0:T(8,128)(2,1)}, u32[]{:S(2)}) copy-start(bf16[256,256]{1,0:T(8,128)(2,1)} %param.9) | copy-start | bytes 393220
  0.6 27.6 %copy-start.2 = (bf16[3,768]{1,0:T(4,128)(2,1)S(1)}, bf16[3,768]{1,0:T(4,128)(2,1)}, u32[]{:S(2)}) copy-start(bf16[3,768]{1,0:T(4,128)(2,1)} %param.6) | copy-start | bytes 13828
  0.7 9.0 %collective-permute-start = (bf16[3,768]{1,0:T(4,128)(2,1)}, bf16[3,768]{1,0:T(4,128)(2,1)S(1)}, u32[]{:S(2)}, u32[]{:S(2)}) collective-permute-start(bf16[3,768]{1,0:T(4,128)(2,1)} %param.6), channel_id=1, source_target_pairs={{0,4},{4,8},{8,12},{12,0},{1,5},{5,9},{9,13},{13,1},{2,6},{6,10},{... | collective-permute-start | bytes 13832 | tf_op jit(solution)/shard_map/ppermute | solution.py:30
  3.7 7.3 %collective-permute-start.2 = (bf16[3,768]{1,0:T(4,128)(2,1)}, bf16[3,768]{1,0:T(4,128)(2,1)S(1)}, u32[]{:S(2)}, u32[]{:S(2)}) collective-permute-start(bf16[3,768]{1,0:T(4,128)(2,1)} %param.6), channel_id=1, source_target_pairs={{0,12},{4,0},{8,4},{12,8},{1,13},{5,1},{9,5},{13,9},{2,14},{6,2},{... | collective-permute-start | bytes 13832 | tf_op jit(solution)/shard_map/ppermute | solution.py:30
  5.8 28.3 %collective-permute-start.1 = (bf16[2,768,64]{1,2,0:T(8,128)(2,1)}, bf16[2,768,64]{1,2,0:T(8,128)(2,1)S(1)}, u32[]{:S(2)}, u32[]{:S(2)}) collective-permute-start(bf16[2,768,64]{1,2,0:T(8,128)(2,1)} %param.8), channel_id=1, source_target_pairs={{0,4},{4,8},{8,12},{12,0},{1,5},{5,9},{9,13},{13,1},{2,6},{6,10},{... | collective-permute-start | bytes 589832 | tf_op jit(solution)/shard_map/ppermute | solution.py:30
  5.8 29.4 %collective-permute-start.3 = (bf16[2,768,64]{1,2,0:T(8,128)(2,1)}, bf16[2,768,64]{1,2,0:T(8,128)(2,1)S(1)}, u32[]{:S(2)}, u32[]{:S(2)}) collective-permute-start(bf16[2,768,64]{1,2,0:T(8,128)(2,1)} %param.8), channel_id=1, source_target_pairs={{0,12},{4,0},{8,4},{12,8},{1,13},{5,1},{9,5},{13,9},{2,14},{6,2},{... | collective-permute-start | bytes 589832 | tf_op jit(solution)/shard_map/ppermute | solution.py:30
  9.6 26.7 %collective-permute-start.5 = (bf16[2,768,64]{1,2,0:T(8,128)(2,1)}, bf16[2,768,64]{1,2,0:T(8,128)(2,1)S(1)}, u32[]{:S(2)}, u32[]{:S(2)}) collective-permute-start(bf16[2,768,64]{1,2,0:T(8,128)(2,1)} %param.8), channel_id=1, source_target_pairs={{0,8},{4,12},{8,0},{12,4},{1,9},{5,13},{9,1},{13,5},{2,10},{6,14},... | collective-permute-start | bytes 589832 | tf_op jit(solution)/shard_map/ppermute | solution.py:30
  9.7 13.2 %collective-permute-start.4 = (bf16[3,768]{1,0:T(4,128)(2,1)S(1)}, bf16[3,768]{1,0:T(4,128)(2,1)S(1)}, u32[]{:S(2)}, u32[]{:S(2)}) collective-permute-start(bf16[3,768]{1,0:T(4,128)(2,1)S(1)} %collective-permute-done), channel_id=1, source_target_pairs={{0,4},{4,8},{8,12},{12,0},{1,5},{5,9},{9,13},{13,1},{2,6},{6,10},{... | collective-permute-start | bytes 13832 | tf_op jit(solution)/shard_map/ppermute | solution.py:30
  24.8 15.1 %all-to-all-start = ((bf16[4,2,768,64]{2,3,1,0:T(8,128)(2,1)}), bf16[4,2,768,64]{2,3,1,0:T(8,128)(2,1)S(1)}, u32[]{:S(2)}, u32[]{:S(2)}) async-start(bf16[4,2,768,64]{2,3,1,0:T(8,128)(2,1)} %broadcast_in_dim.2), calls=%async_computation | async-start | bytes 1572864 | tf_op jit(solution)/shard_map/all_to_all | solution.py:87
  28.4 4.7 %copy-start.1 = (bf16[2,768,64]{1,2,0:T(8,128)(2,1)S(1)}, bf16[2,768,64]{1,2,0:T(8,128)(2,1)}, u32[]{:S(2)}) copy-start(bf16[2,768,64]{1,2,0:T(8,128)(2,1)} %param.8) | copy-start | bytes 589828
  36.3 8.7 %copy-start.4 = (bf16[2]{0:T(256)(128)(2,1)S(1)}, bf16[2]{0:T(256)(128)(2,1)}, u32[]{:S(2)}) copy-start(bf16[2]{0:T(256)(128)(2,1)} %constant.54.clone) | copy-start | bytes 16
  39.9 5.1 %collective-permute-start.6 = (bf16[64,2,768]{2,0,1:T(8,128)(2,1)S(1)}, bf16[64,2,768]{2,0,1:T(8,128)(2,1)S(1)}, u32[]{:S(2)}, u32[]{:S(2)}) collective-permute-start(bf16[64,2,768]{2,0,1:T(8,128)(2,1)S(1)} %bitcast.43), channel_id=1, source_target_pairs={{0,1},{1,2},{2,3},{3,0},{4,5},{5,6},{6,7},{7,4},{8,9},{9,10},{10,1... | collective-permute-start | bytes 589832 | tf_op jit(solution)/shard_map/ppermute | solution.py:18
  45.0 6.8 %collective-permute-start.7 = (bf16[64,2,768]{2,0,1:T(8,128)(2,1)S(1)}, bf16[64,2,768]{2,0,1:T(8,128)(2,1)S(1)}, u32[]{:S(2)}, u32[]{:S(2)}) collective-permute-start(bf16[64,2,768]{2,0,1:T(8,128)(2,1)S(1)} %collective-permute-done.6), channel_id=1, source_target_pairs={{0,1},{1,2},{2,3},{3,0},{4,5},{5,6},{6,7},{7,4},{8,9},{9,10},{10,1... | collective-permute-start | bytes 589832 | tf_op jit(solution)/shard_map/ppermute | solution.py:18
  45.7 6.4 %collective-permute-start.10 = (f32[64,256]{1,0:T(8,128)S(1)}, f32[64,256]{1,0:T(8,128)S(1)}, u32[]{:S(2)}, u32[]{:S(2)}) collective-permute-start(f32[64,256]{1,0:T(8,128)S(1)} %reshape.69), channel_id=1, source_target_pairs={{0,4},{4,8},{8,12},{12,0},{1,5},{5,9},{9,13},{13,1},{2,6},{6,10},{... | collective-permute-start | bytes 196616 | tf_op jit(solution)/shard_map/ppermute | solution.py:30
  47.0 8.0 %collective-permute-start.11 = (f32[64,256]{1,0:T(8,128)S(1)}, f32[64,256]{1,0:T(8,128)S(1)}, u32[]{:S(2)}, u32[]{:S(2)}) collective-permute-start(f32[64,256]{1,0:T(8,128)S(1)} %reshape.69), channel_id=1, source_target_pairs={{0,8},{4,12},{8,0},{12,4},{1,9},{5,13},{9,1},{13,5},{2,10},{6,14},... | collective-permute-start | bytes 196616 | tf_op jit(solution)/shard_map/ppermute | solution.py:30
  48.9 6.0 %collective-permute-start.9 = (f32[64,256]{1,0:T(8,128)S(1)}, f32[64,256]{1,0:T(8,128)S(1)}, u32[]{:S(2)}, u32[]{:S(2)}) collective-permute-start(f32[64,256]{1,0:T(8,128)S(1)} %reshape.69), channel_id=1, source_target_pairs={{0,12},{4,0},{8,4},{12,8},{1,13},{5,1},{9,5},{13,9},{2,14},{6,2},{... | collective-permute-start | bytes 196616 | tf_op jit(solution)/shard_map/ppermute | solution.py:30
  51.8 5.1 %collective-permute-start.8 = (bf16[64,2,768]{2,0,1:T(8,128)(2,1)S(1)}, bf16[64,2,768]{2,0,1:T(8,128)(2,1)S(1)}, u32[]{:S(2)}, u32[]{:S(2)}) collective-permute-start(bf16[64,2,768]{2,0,1:T(8,128)(2,1)S(1)} %collective-permute-done.7), channel_id=1, source_target_pairs={{0,1},{1,2},{2,3},{3,0},{4,5},{5,6},{6,7},{7,4},{8,9},{9,10},{10,1... | collective-permute-start | bytes 589832 | tf_op jit(solution)/shard_map/ppermute | solution.py:18
  56.9 0.8 %copy-start.3 = (f32[64]{0:T(128)S(1)}, f32[64]{0:T(128)}, u32[]{:S(2)}) copy-start(f32[64]{0:T(128)} %param.10) | copy-start | bytes 772
